TPU v7x, 32 devices: a whole 2x2x4 slice. The times are simulated.
32 devices in a mesh: dp: 8 (over z, x), expert: 4 (over y, core).
Axes of the slice: x: 2, y: 2, z: 4, core: 2. Of those that a mesh axis runs over, the one named last changes fastest.
Arguments:
- hidden: bfloat16 [2048, 2304], P(('dp', 'expert')), may hold values from -6 to 6
- tree_qkv: bfloat16 [2048, 6912], P(('dp', 'expert')), may hold values from -7 to 7
- prompt_kv: bfloat16 [8, 512, 4608], P('dp', 'expert'), may hold values from -6 to 6
- prompt_len: int32 [8], P('dp'), may hold values from 128 to 512, as said below
- private_kv: bfloat16 [32, 512, 4608], P(('dp', 'expert')), may hold values from -6 to 6
- priv_len: int32 [32], P(('dp', 'expert')), may hold values from 1 to 512, as said below
- parents: int32 [32, 64], P(('dp', 'expert')), may hold values from -1 to 62, as said below
- leaf: int32 [32], P(('dp', 'expert')), may hold values from 0 to 63
- w_out: bfloat16 [2304, 2304], replicated, may hold values from -3 to 3
- norm_gain: float32 [2304], replicated, may hold values from 0.1 to 1.9
- w_router: bfloat16 [2304, 4], replicated, as said below
- routes: int32 [2048, 2], P(('dp', 'expert')), may hold values from 0 to 3, all different within a row; in each aligned block of 64 rows (0 to 63, 64 to 127, ...) at most 48 rows name the same one
- w_gate_up: bfloat16 [4, 2, 2304, 5760], P('expert', None, None, 'dp'), may hold values from -0.125 to 0.125
- w_down: bfloat16 [4, 5760, 2304], P('expert', 'dp'), may hold values from -0.15625 to 0.15625
Outputs:
- layer_out: bfloat16 [2048, 2304], P(('dp', 'expert'))
- accepted_kv: bfloat16 [32, 64, 4608], P(('dp', 'expert'))
Inputs may be any that keep to these rules, and one draw needn't show every extreme that they name: `routes`: the rows of one device (aligned blocks of 64 rows) name each expert at most 48 times; the two experts of a row differ. `prompt_len`: some group's length is exactly 512. `priv_len`: some request's length is exactly 512. parents[r, 0] = -1; for t >= 1, max(0, t - 8) <= parents[r, t] <= t - 1. `w_router`: entries lie within 3 / sqrt(27648) of zero.
All inputs are finite; a program needn't handle non-finite values.
Results may differ from a plain program's by a relative error of at most 0.014.
Values may be sent and summed in bfloat16 or wider, within the bound.
No kernel may reach another device: no remote copies, remote signals or barrier semaphores. Data moves between devices by JAX's collectives and lax.ppermute only.
A program may use at most 128 MiB of HBM per device.

v0:
```python
import math
import jax
import jax.numpy as jnp
from jax import lax
from jax.sharding import PartitionSpec as P

H = 36
HD = 64
TREE = 64
REQ_DEV = 1
NEG = -1e30
EPS = 1e-05
HIGH = lax.Precision.HIGHEST


def closure(parents):
    count = parents.shape[-1]
    columns = jnp.arange(count, dtype=jnp.int32)
    reached = (parents[:, :, None] == columns[None, None, :]).astype(jnp.float32) + jnp.eye(
        count, dtype=jnp.float32
    )[None]
    for sweeps in range((count - 1).bit_length()):
        reached = jnp.minimum(jnp.einsum("rij,rjk->rik", reached, reached, precision=HIGH), 1.0)
    return reached


def compact(reach_one, leaf_one, kv_one):
    count = reach_one.shape[0]
    marked = jnp.sum(
        jnp.where(jnp.arange(count, dtype=jnp.int32)[:, None] == leaf_one, reach_one, 0.0), axis=0
    )
    earlier = (
        jnp.arange(count, dtype=jnp.int32)[None, :] < jnp.arange(count, dtype=jnp.int32)[:, None]
    ).astype(jnp.float32)
    ordinal = jnp.dot(earlier, marked, precision=HIGH)
    slot_ids = jnp.arange(count, dtype=jnp.int32).astype(jnp.float32)
    chosen = jnp.where(slot_ids[:, None] == ordinal[None, :], marked[None, :], 0.0)
    return jnp.dot(chosen.astype(jnp.bfloat16), kv_one, preferred_element_type=jnp.float32).astype(
        jnp.bfloat16
    )


def partial_attention(query_matrix_rows, cache_rows, allowed):
    features = cache_rows.shape[1] // 2
    slots = cache_rows.shape[0]
    key_matrix_rows = cache_rows[:, :features].reshape(slots, H, HD)
    value_matrix_rows = cache_rows[:, features:].reshape(slots, H, HD)
    attention_score_scale = 1.0 / math.sqrt(HD)
    attention_scores = (
        jnp.einsum(
            "was,zas->waz", query_matrix_rows, key_matrix_rows, preferred_element_type=jnp.float32
        )
        * attention_score_scale
    )
    widened = allowed[:, None, :]
    attention_scores = jnp.where(widened, attention_scores, NEG)
    maxima = jnp.max(attention_scores, axis=-1)
    attention_weights = jnp.where(widened, jnp.exp(attention_scores - maxima[..., None]), 0.0)
    totals = jnp.sum(attention_weights, axis=-1)
    weighted_sum = jnp.einsum(
        "ubj,jbx->ubx",
        attention_weights.astype(jnp.bfloat16),
        value_matrix_rows,
        preferred_element_type=jnp.float32,
    )
    return (maxima, totals, weighted_sum)


def join_parts(first_part, second_part):
    highest = jnp.maximum(first_part[0], second_part[0])
    scale_first = jnp.exp(first_part[0] - highest)
    scale_second = jnp.exp(second_part[0] - highest)
    totals = first_part[1] * scale_first + second_part[1] * scale_second
    weighted_sum = first_part[2] * scale_first[..., None] + second_part[2] * scale_second[..., None]
    return (highest, totals, weighted_sum)


def as_rows(part_state, row_count):
    return (
        part_state[0].reshape(row_count, H),
        part_state[1].reshape(row_count, H),
        part_state[2].reshape(row_count, H, HD),
    )


def local(
    hidden,
    tree_qkv,
    prompt_kv,
    prompt_len,
    private_kv,
    priv_len,
    parents,
    leaf,
    w_out,
    norm_gain,
    w_router,
    routes,
    w_gate_up,
    w_down,
):
    row_count = hidden.shape[0]
    features = hidden.shape[1]
    query_vectors = tree_qkv[:, :features].reshape(row_count, H, HD)
    new_kv = tree_qkv[:, features:]
    reached = closure(parents)
    grouped_q = query_vectors.reshape(REQ_DEV, TREE, H, HD)
    grouped_kv = new_kv.reshape(REQ_DEV, TREE, 2 * features)
    tree_part = jax.vmap(partial_attention)(grouped_q, grouped_kv, reached > 0.5)
    private_slots = jnp.arange(private_kv.shape[1], dtype=jnp.int32)
    private_ok = jnp.broadcast_to(
        (private_slots[None, :] < priv_len[:, None])[:, None, :],
        (REQ_DEV, TREE, private_kv.shape[1]),
    )
    private_part = jax.vmap(partial_attention)(grouped_q, private_kv, private_ok)
    local_state = join_parts(as_rows(tree_part, row_count), as_rows(private_part, row_count))
    prompt_limit = prompt_len[0]
    start_state = (
        jnp.full((row_count, H), NEG, jnp.float32),
        jnp.zeros((row_count, H), jnp.float32),
        jnp.zeros((row_count, H, HD), jnp.float32),
    )
    shard_rows = lax.all_gather(prompt_kv, "expert", axis=1, tiled=True)
    piece_len = shard_rows.shape[1]
    places = jnp.arange(piece_len, dtype=jnp.int32)
    allowed = jnp.broadcast_to((places < prompt_limit)[None, :], (row_count, piece_len))
    prompt_state = join_parts(start_state, partial_attention(query_vectors, shard_rows[0], allowed))
    final_state = join_parts(local_state, prompt_state)
    context = (
        (final_state[2] / final_state[1][..., None])
        .reshape(row_count, features)
        .astype(jnp.bfloat16)
    )
    attended = jnp.dot(context, w_out, preferred_element_type=jnp.float32)
    middle = (hidden.astype(jnp.float32) + attended).astype(jnp.bfloat16)
    middle32 = middle.astype(jnp.float32)
    normed = (
        middle32 * lax.rsqrt(jnp.mean(middle32 * middle32, axis=1, keepdims=True) + EPS) * norm_gain
    ).astype(jnp.bfloat16)
    logits = jnp.dot(normed, w_router, preferred_element_type=jnp.float32)
    experts = w_router.shape[1]
    choose = routes[:, :, None] == jnp.arange(experts, dtype=jnp.int32)[None, None, :]
    picked = jnp.sum(jnp.where(choose, logits[:, None, :], 0.0), axis=2)
    gate_first = jax.nn.sigmoid(picked[:, 0] - picked[:, 1])
    gate_second = jax.nn.sigmoid(picked[:, 1] - picked[:, 0])
    capacity = 3 * row_count // experts
    onehot = choose.reshape(2 * row_count, experts).astype(jnp.float32)
    assign_ids = jnp.arange(2 * row_count, dtype=jnp.int32)
    earlier = (assign_ids[None, :] < assign_ids[:, None]).astype(jnp.float32)
    before = jnp.dot(earlier, onehot, precision=HIGH)
    slot_rank = jnp.sum(before * onehot, axis=1).astype(jnp.int32)
    target = routes.reshape(2 * row_count) * capacity + slot_rank
    select = (jnp.arange(experts * capacity, dtype=jnp.int32)[:, None] == target[None, :]).astype(
        jnp.bfloat16
    )
    doubled = jnp.repeat(normed, 2, axis=0)
    outgoing = (
        jnp.dot(select, doubled, preferred_element_type=jnp.float32)
        .astype(jnp.bfloat16)
        .reshape(experts, capacity, features)
    )
    gate_cols = w_gate_up[0, 0]
    up_cols = w_gate_up[0, 1]
    down_rows = w_down[0]
    arrived = lax.all_to_all(outgoing, "expert", split_axis=0, concat_axis=0, tiled=True)
    pooled = lax.all_gather(arrived.reshape(experts * capacity, features), "dp", axis=0, tiled=True)
    gate_act = jnp.dot(pooled, gate_cols, preferred_element_type=jnp.float32)
    upper = jnp.dot(pooled, up_cols, preferred_element_type=jnp.float32)
    hidden_units = (jax.nn.silu(gate_act) * upper).astype(jnp.bfloat16)
    summed_rows = lax.psum_scatter(
        jnp.dot(hidden_units, down_rows, preferred_element_type=jnp.float32).astype(jnp.bfloat16),
        "dp",
        scatter_dimension=0,
        tiled=True,
    ).astype(jnp.float32)
    returned = lax.all_to_all(
        summed_rows.reshape(experts, capacity, features).astype(jnp.bfloat16),
        "expert",
        split_axis=0,
        concat_axis=0,
        tiled=True,
    ).astype(jnp.float32)
    flat_back = returned.reshape(experts * capacity, features)
    fetched = jnp.take(flat_back, target, axis=0).reshape(row_count, 2, features)
    layer_out = (
        middle32 + gate_first[:, None] * fetched[:, 0] + gate_second[:, None] * fetched[:, 1]
    ).astype(jnp.bfloat16)
    accepted_kv = jax.vmap(compact)(reached, leaf, grouped_kv)
    return (layer_out, accepted_kv)


def solution(mesh):
    placed = (
        P(("dp", "expert"), None),
        P(("dp", "expert"), None),
        P("dp", "expert", None),
        P("dp"),
        P(("dp", "expert"), None, None),
        P(("dp", "expert")),
        P(("dp", "expert"), None),
        P(("dp", "expert")),
        P(),
        P(),
        P(),
        P(("dp", "expert"), None),
        P("expert", None, None, "dp"),
        P("expert", "dp", None),
    )
    return jax.shard_map(
        local,
        mesh=mesh,
        in_specs=placed,
        out_specs=(P(("dp", "expert"), None), P(("dp", "expert"), None, None)),
        check_vma=False,
    )
```

profile of v0, /device:TPU:0, one launch (start us, length us, event | category | flops | bytes accessed | tf_op | source)
XLA Modules:
  0.0 406.6 jit_solution(13038210003141550185)
XLA Ops:
  7.2 0.7 all-gather.3.cloned.1.call-update
  8.0 1.0 fusion.86
  9.0 0.2 convolution_minimum_fusion.5
  9.1 0.2 convolution_minimum_fusion.4
  9.3 0.2 convolution_minimum_fusion.3
  9.5 0.2 convolution_minimum_fusion.2
  9.6 0.2 convolution_minimum_fusion.1
  9.8 0.2 broadcast_compare_fusion
  10.1 1.7 slice.46
  11.8 2.3 reshape.469
  14.1 1.1 slice_bitcast_fusion.2
  15.2 0.9 fusion.112
  16.0 2.3 reshape.468
  19.0 5.4 %fusion.110 = (bf16[1,512,2304]{2,1,0:T(8,128)(2,1)}, bf16[1,512,2304]{2,1,0:T(8,128)(2,1)}) fusion(bf16[1,512,4608]{2,1,0:T(8,128)(2,1)} %param.18), kind=kLoop, calls=%fused_computation.152 | loop fusion | bytes 9437184 | tf_op jit(solution)/shard_map/vmap()/slice | solution.py:47
  24.4 4.3 %copy.66 = bf16[1,512,2304]{1,2,0:T(8,128)(2,1)} copy(bf16[1,512,2304]{2,1,0:T(8,128)(2,1)} %get-tuple-element.8) | data formatting | bytes 4718592 | tf_op jit(solution)/shard_map/vmap()/slice | solution.py:46
  29.4 4.3 %copy.68 = bf16[1,512,2304]{1,2,0:T(8,128)(2,1)} copy(bf16[1,512,2304]{2,1,0:T(8,128)(2,1)} %get-tuple-element.7) | data formatting | bytes 4718592 | tf_op jit(solution)/shard_map/vmap()/slice | solution.py:47
  33.7 2.3 reshape.471
  35.9 0.1 copy.73
  36.0 0.1 reshape.479
  36.2 0.1 fusion.64
  36.4 1.9 fusion.113
  38.3 0.3 fusion.65
  38.6 0.7 copy-done.11
  39.3 0.9 bitcast_reduce_fusion.1
  40.2 2.2 copy-done.2
  42.4 1.4 fusion.7
  43.8 5.9 %all-gather.3.cloned.1.call-done = bf16[1,512,4608]{2,1,0:T(8,128)(2,1)} async-done(((bf16[1,128,4608]{2,1,0:T(8,128)(2,1)}), bf16[1,512,4608]{2,1,0:T(8,128)(2,1)}) %all-gather.3.cloned.1.call-update) | async-done | bytes 4718608 | tf_op jit(solution)/shard_map/all_gather | solution.py:123
  49.7 4.9 %fusion.111 = (bf16[512,2304]{1,0:T(8,128)(2,1)}, bf16[512,2304]{1,0:T(8,128)(2,1)}) fusion(bf16[512,4608]{1,0:T(8,128)(2,1)} %bitcast.201), kind=kLoop, calls=%fused_computation.153 | loop fusion | bytes 9437184 | tf_op jit(solution)/shard_map/slice | solution.py:46
  54.6 4.3 %copy.69 = bf16[512,2304]{0,1:T(8,128)(2,1)} copy(bf16[512,2304]{1,0:T(8,128)(2,1)} %get-tuple-element.9) | data formatting | bytes 4718592 | tf_op jit(solution)/shard_map/slice | solution.py:46
  58.9 4.3 %copy.71 = bf16[512,2304]{0,1:T(8,128)(2,1)} copy(bf16[512,2304]{1,0:T(8,128)(2,1)} %get-tuple-element.10) | data formatting | bytes 4718592 | tf_op jit(solution)/shard_map/slice | solution.py:47
  63.2 2.9 bitcast_reduce_fusion
  66.0 1.5 fusion.9
  67.6 0.1 copy-done.9
  67.7 1.4 fusion.59
  69.1 0.3 copy-done.10
  69.4 1.9 fusion.56
  71.3 1.8 fusion.62
  73.0 1.2 copy.72
  74.3 2.2 convert_element_type.146
  76.4 6.1 %multiply_reduce_fusion = (f32[64]{0:T(128)S(1)}, f32[64,2304]{1,0:T(8,128)S(1)}) fusion(bf16[64,2304]{1,0:T(8,128)(2,1)} %convert_element_type.146, bf16[2304,2304]{1,0:T(8,128)(2,1)} %param.22, bf16[64,2304]{1,0:T(8,128)(2,1)} %param.14), kind=kOutput, calls=%fused_computation.86 | convolution fusion | flops 680361920 | bytes 11796736 | tf_op jit(solution)/shard_map/dot_general | solution.py:134
  82.6 0.8 copy-done.4
  83.4 0.1 multiply_convert_fusion.1
  83.5 0.7 copy-done.6
  84.2 1.1 broadcast_in_dim.163
  85.4 2.7 reshape.480
  88.1 1.4 convolution_convert_fusion.2
  89.5 15.8 %all_to_all.10 = bf16[4,48,2304]{2,1,0:T(8,128)(2,1)} all-to-all(bf16[4,48,2304]{2,1,0:T(8,128)(2,1)S(1)} %bitcast.203), channel_id=1, replica_groups=mesh['dp'=8,'expert'=4] {'expert'}, dimensions={0} | all-to-all | bytes 1769472 | tf_op jit(solution)/shard_map/all_to_all | solution.py:165
  105.4 108.4 %all-gather.5.cloned.1.call-done = bf16[1536,2304]{1,0:T(8,128)(2,1)} async-done(((bf16[192,2304]{1,0:T(8,128)(2,1)}), bf16[1536,2304]{1,0:T(8,128)(2,1)}) %all-gather.5.cloned.1.call-update) | async-done | bytes 7077904 | tf_op jit(solution)/shard_map/all_gather | solution.py:166
  213.8 10.5 %fusion.15 = f32[1536,720]{0,1:T(8,128)} fusion(bf16[1536,2304]{1,0:T(8,128)(2,1)} %all-gather.5.cloned.1.call-done, bf16[1,2,2304,720]{2,3,1,0:T(8,128)(2,1)} %param.26), kind=kOutput, calls=%fused_computation.25 | convolution fusion | flops 5096079360 | bytes 14819328 | tf_op jit(solution)/shard_map/dot_general | solution.py:167
  224.3 20.2 %convolution_convert_fusion = bf16[1536,2304]{1,0:T(8,128)(2,1)} fusion(bf16[1,720,2304]{2,1,0:T(8,128)(2,1)S(1)} %copy-done, f32[1536,720]{0,1:T(8,128)} %fusion.15, bf16[1536,2304]{1,0:T(8,128)(2,1)} %all-gather.5.cloned.1.call-done, bf16[1,2,2304,720]{2,3,1,0:T(8,128)(2,1)} %param.26), kind=kOutput, calls=%fused_computation.1 | convolution fusion | flops 10202333184 | bytes 25214976 | tf_op jit(solution)/shard_map/dot_general | solution.py:171
  244.5 0.1 copy.75
  244.6 0.1 mul.221
  244.7 0.1 convert_element_type.151
  245.7 0.1 convolution_bitcast_fusion.1
  245.8 1.2 fusion
  247.1 124.9 %reduce-scatter.2.cloned.1.call-done = bf16[192,2304]{1,0:T(8,128)(2,1)} async-done(((bf16[1536,2304]{1,0:T(8,128)(2,1)}), bf16[192,2304]{1,0:T(8,128)(2,1)}) %reduce-scatter.2.cloned.1.call-update) | async-done | bytes 884752 | tf_op jit(solution)/shard_map/reduce_scatter | solution.py:170
  371.9 3.5 all-to-all-start.1
  375.5 0.2 fusion.114
  375.7 12.4 %all-to-all-done.1 = bf16[4,48,2304]{2,1,0:T(8,128)(2,1)S(1)} async-done(((bf16[4,48,2304]{2,1,0:T(8,128)(2,1)}), bf16[4,48,2304]{2,1,0:T(8,128)(2,1)S(1)}, u32[]{:S(2)}, u32[]{:S(2)}) %all-to-all-start.1) | async-done | bytes 884768 | tf_op jit(solution)/shard_map/all_to_all | solution.py:176
  388.1 1.4 bitcast_convert_fusion
  389.5 4.2 %gather_fusion = f32[128,2304]{1,0:T(8,128)} fusion(f32[192,2304]{1,0:T(8,128)} %bitcast_convert_fusion, s32[1024]{0:T(1024)S(1)} %pad_clamp_fusion), kind=kCustom, calls=%fused_computation | custom fusion | bytes 2359808 | tf_op jit(solution)/shard_map/jit(_take)/gather | solution.py:184
  393.7 2.9 gather.7
  396.6 1.4 copy_select_fusion
  398.0 2.0 fusion.71
  (55 shorter events, 0.6 us)
Async XLA Ops:
  7.2 217.1 %copy-start = (bf16[1,720,2304]{2,1,0:T(8,128)(2,1)S(1)}, bf16[1,720,2304]{2,1,0:T(8,128)(2,1)}, u32[]{:S(2)}) copy-start(bf16[1,720,2304]{2,1,0:T(8,128)(2,1)} %param.27) | copy-start | bytes 9953284
  7.2 42.6 %all-gather.3.cloned.1.call-start = ((), (), s32[]{:S(2)}) async-start(), calls=%async_computation.3 | async-start | bytes 5898240 | tf_op jit(solution)/shard_map/all_gather | solution.py:123
  7.9 205.9 %all-gather.5.cloned.1.call-start = ((), (), s32[]{:S(2)}) async-start(), calls=%async_computation.4 | async-start | bytes 7962624 | tf_op jit(solution)/shard_map/all_gather | solution.py:166
  28.7 7.2 %copy-start.15 = (s32[64,2]{0,1:T(2,128)S(1)}, s32[64,2]{0,1:T(2,128)}, u32[]{:S(2)}) copy-start(s32[64,2]{0,1:T(2,128)} %param.25) | copy-start | bytes 1540
  36.2 3.1 copy-start.3
  36.2 3.1 copy-start.5
  38.3 1.0 copy-start.11
  40.2 2.2 copy-start.2
  63.2 4.4 %slice-start = ((s8[4718592]{0:T(1024)(128)(4,1)}), s8[4194304]{0:T(1024)(128)(4,1)S(1)}, s32[]{:S(2)}) async-start(s8[4718592]{0:T(1024)(128)(4,1)} %bitcast.197), calls=%async_computation.6 | async-start | bytes 8388608
  63.2 4.4 %slice-start.1 = ((s8[4718592]{0:T(1024)(128)(4,1)}), s8[524288]{0:T(1024)(128)(4,1)S(1)}, s32[]{:S(2)}) async-start(s8[4718592]{0:T(1024)(128)(4,1)} %bitcast.197), calls=%async_computation.7 | async-start | bytes 1048576
  66.0 1.7 copy-start.9
  67.7 1.7 copy-start.10
  69.4 1.9 copy-start.12
  69.4 1.9 copy-start.13
  76.4 7.0 %copy-start.16 = (f32[2304]{0:T(1024)S(1)}, f32[2304]{0:T(1024)}, u32[]{:S(2)}) copy-start(f32[2304]{0:T(1024)} %param.23) | copy-start | bytes 27652
  82.6 0.8 copy-start.4
  83.5 0.7 copy-start.6
  105.4 266.6 %reduce-scatter.2.cloned.1.call-start = ((), (), s32[]{:S(2)}) async-start(), calls=%async_computation.5 | async-start | bytes 7962624 | tf_op jit(solution)/shard_map/reduce_scatter | solution.py:170
  244.4 1.4 copy-start.8
  244.4 131.0 %copy-start.7 = (bf16[64,2304]{1,0:T(8,128)(2,1)S(1)}, bf16[64,2304]{1,0:T(8,128)(2,1)}, u32[]{:S(2)}) copy-start(bf16[64,2304]{1,0:T(8,128)(2,1)} %copy-done.6) | copy-start | bytes 884740
  244.4 131.0 %copy-start.14 = (bf16[2304,4]{0,1:T(4,128)(2,1)S(1)}, bf16[2304,4]{0,1:T(4,128)(2,1)}, u32[]{:S(2)}) copy-start(bf16[2304,4]{0,1:T(4,128)(2,1)} %param.24) | copy-start | bytes 55300
  371.9 16.2 %all-to-all-start.1 = ((bf16[4,48,2304]{2,1,0:T(8,128)(2,1)}), bf16[4,48,2304]{2,1,0:T(8,128)(2,1)S(1)}, u32[]{:S(2)}, u32[]{:S(2)}) async-start(bf16[4,48,2304]{2,1,0:T(8,128)(2,1)} %bitcast.206), calls=%async_computation.2 | async-start | bytes 1769472 | tf_op jit(solution)/shard_map/all_to_all | solution.py:176
  389.5 10.5 %copy-start.1 = (bf16[1,720,2304]{2,1,0:T(8,128)(2,1)S(1)}, bf16[1,720,2304]{2,1,0:T(8,128)(2,1)}, u32[]{:S(2)}) copy-start(bf16[1,720,2304]{2,1,0:T(8,128)(2,1)} %param.27) | copy-start | bytes 9953284
Sparse Core Ops, SparseCore 0:
  9.5 40.1 all-gather.2
  105.5 108.2 all-gather.4
  244.6 127.3 reduce-scatter.1
where the time goes:
time: 408 us; the launch traced here: 407 us
  waiting for transfers between devices  252 us (62%)
  local copies, waits for them, and re-layouts  57.9 us (14%)
  matrix products  51.5 us (13%)
  between operations  16.1 us (4%)
  blocking collectives  15.8 us (4%)
  other arithmetic  9.36 us (2%)
    reduce_scatter x1, waiting for transfers between devices, local(): lax.psum_scatter(jnp.dot(hidden_units, down_rows, preferred_element_type=...  125 us
    all_gather x1, waiting for transfers between devices, local(): lax.all_gather(arrived.reshape(experts * capacity, features), 'dp', axis=...  108 us
    dot_general x1, matrix products, local(): jnp.dot(hidden_units, down_rows, preferred_element_type=jnp.float32)  20.2 us
    all_to_all x1, blocking collectives, local(): lax.all_to_all(outgoing, 'expert', split_axis=0, concat_axis=0, tiled=True)  15.8 us
    slice x4, local copies, waits for them, and re-layouts, partial_attention(): value_matrix_rows = cache_rows[:, features:].reshape(slots, H, HD)  14.8 us
    slice x3, local copies, waits for them, and re-layouts, partial_attention(): key_matrix_rows = cache_rows[:, :features].reshape(slots, H, HD)  13.4 us
    all_to_all x1, waiting for transfers between devices, local(): lax.all_to_all(summed_rows.reshape(experts, capacity, features).astype(jn...  12.4 us
    dot_general x1, matrix products, local(): gate_act = jnp.dot(pooled, gate_cols, preferred_element_type=jnp.float32)  10.5 us
  transfers between devices with their start and end apart: 4, of which 4 were waited for; matrix products, arithmetic and copies ran while one was open for 8% of the time, Pallas kernels for 0%

commit v1 on v0

--- a/solution.py
+++ b/solution.py
@@ -11,6 +11,24 @@
 NEG = -1e30
 EPS = 1e-05
 HIGH = lax.Precision.HIGHEST
+
+
+def joined_along(tiles, dim):
+    dims = list(tiles.shape[1:])
+    dims[dim] *= tiles.shape[0]
+    return jnp.moveaxis(tiles, 0, dim).reshape(dims)
+
+
+def collected_by_bits(x, axis):
+    size = lax.axis_size(axis)
+    parts = x[None]
+    for level in range(size.bit_length() - 1):
+        stride = 1 << level
+        other = lax.ppermute(parts, axis, [(i, i ^ stride) for i in range(size)])
+        both = jnp.stack([parts, other])
+        upper = lax.axis_index(axis) >> level & 1
+        parts = jnp.where(upper == 0, both, both[::-1]).reshape(-1, *x.shape)
+    return parts
 
 
 def closure(parents):
@@ -163,7 +181,8 @@
     up_cols = w_gate_up[0, 1]
     down_rows = w_down[0]
     arrived = lax.all_to_all(outgoing, "expert", split_axis=0, concat_axis=0, tiled=True)
-    pooled = lax.all_gather(arrived.reshape(experts * capacity, features), "dp", axis=0, tiled=True)
+    x = arrived.reshape(experts * capacity, features)
+    pooled = joined_along(collected_by_bits(x, "dp"), 0)
     gate_act = jnp.dot(pooled, gate_cols, preferred_element_type=jnp.float32)
     upper = jnp.dot(pooled, up_cols, preferred_element_type=jnp.float32)
     hidden_units = (jax.nn.silu(gate_act) * upper).astype(jnp.bfloat16)

time: 408 us -> 535 us (1.31)
  waiting for transfers between devices: 252 us -> 353 us
  other arithmetic: 9.36 us -> 26.9 us
  starting transfers between devices: 3.62 us -> 9.88 us
    ppermute x0 -> x3, waiting for transfers between devices: none -> 209 us  [collected_by_bits(): other = lax.ppermute(parts, axis, [(i, i ^ stride) for i in range(size)])]
    all_gather x1 -> x0, waiting for transfers between devices: 108 us -> none  [local(): lax.all_gather(arrived.reshape(experts * capacity, features), 'dp', axis=...]
    another operation x0 -> x4, other arithmetic: none -> 9.76 us  [collected_by_bits(): both = jnp.stack([parts, other])]
    select_n x0 -> x2, other arithmetic: none -> 6.72 us  [collected_by_bits(): parts = jnp.where(upper == 0, both, both[::-1]).reshape(-1, *x.shape)]
    ppermute x0 -> x3, starting transfers between devices: none -> 5.37 us  [collected_by_bits(): other = lax.ppermute(parts, axis, [(i, i ^ stride) for i in range(size)])]
  transfers between devices with their start and end apart: 4 -> 6, of which waited for: 4 -> 6; matrix products, arithmetic and copies ran while one was open for 8% -> 7% of each run, Pallas kernels for 0% -> 0%
where the time goes in v1:
time: 535 us; the launch traced here: 534 us
  waiting for transfers between devices  353 us (66%)
  local copies, waits for them, and re-layouts  57.7 us (11%)
  matrix products  53.5 us (10%)
  other arithmetic  26.9 us (5%)
  between operations  16.4 us (3%)
  blocking collectives  15.8 us (3%)
  starting transfers between devices  9.88 us (2%)
    ppermute x3, waiting for transfers between devices, collected_by_bits(): other = lax.ppermute(parts, axis, [(i, i ^ stride) for i in range(size)])  209 us
    reduce_scatter x1, waiting for transfers between devices, local(): lax.psum_scatter(jnp.dot(hidden_units, down_rows, preferred_element_type=...  126 us
    dot_general x1, matrix products, local(): jnp.dot(hidden_units, down_rows, preferred_element_type=jnp.float32)  20.1 us
    all_to_all x1, blocking collectives, local(): lax.all_to_all(outgoing, 'expert', split_axis=0, concat_axis=0, tiled=True)  15.8 us
    slice x4, local copies, waits for them, and re-layouts, partial_attention(): value_matrix_rows = cache_rows[:, features:].reshape(slots, H, HD)  14.9 us
    slice x3, local copies, waits for them, and re-layouts, partial_attention(): key_matrix_rows = cache_rows[:, :features].reshape(slots, H, HD)  13.5 us
    all_to_all x1, waiting for transfers between devices, local(): lax.all_to_all(summed_rows.reshape(experts, capacity, features).astype(jn...  11.5 us
  transfers between devices with their start and end apart: 6, of which 6 were waited for; matrix products, arithmetic and copies ran while one was open for 7% of the time, Pallas kernels for 0%

profile of v1, /device:TPU:0, one launch (start us, length us, event | category | flops | bytes accessed | tf_op | source)
XLA Modules:
  0.0 533.7 jit_solution(3193009119544520275)
XLA Ops:
  7.2 0.7 all-gather.2.cloned.1.call-update
  8.0 1.0 fusion.88
  9.0 0.2 convolution_minimum_fusion.5
  9.5 0.2 convolution_minimum_fusion.2
  9.6 0.2 convolution_minimum_fusion.1
  9.8 0.2 broadcast_compare_fusion
  10.1 1.7 slice.46
  11.8 2.3 reshape.472
  14.1 1.1 slice_bitcast_fusion.2
  15.2 0.9 fusion.114
  16.0 2.3 reshape.471
  19.0 5.4 %fusion.112 = (bf16[1,512,2304]{2,1,0:T(8,128)(2,1)}, bf16[1,512,2304]{2,1,0:T(8,128)(2,1)}) fusion(bf16[1,512,4608]{2,1,0:T(8,128)(2,1)} %param.18), kind=kLoop, calls=%fused_computation.160 | loop fusion | bytes 9437184 | tf_op jit(solution)/shard_map/vmap()/slice | solution.py:65
  24.4 4.3 copy.66
  29.4 4.3 copy.68
  33.7 2.3 reshape.474
  36.4 1.9 fusion.115
  38.3 0.3 fusion.67
  38.6 0.7 copy-done.8
  39.3 0.9 bitcast_reduce_fusion.1
  40.2 2.2 copy-done.1
  42.4 1.4 fusion.7
  43.8 5.9 %all-gather.2.cloned.1.call-done = bf16[1,512,4608]{2,1,0:T(8,128)(2,1)} async-done(((bf16[1,128,4608]{2,1,0:T(8,128)(2,1)}), bf16[1,512,4608]{2,1,0:T(8,128)(2,1)}) %all-gather.2.cloned.1.call-update) | async-done | bytes 4718608 | tf_op jit(solution)/shard_map/all_gather | solution.py:141
  49.7 4.9 fusion.113
  54.6 4.3 copy.69
  58.9 4.3 copy.71
  63.2 2.9 bitcast_reduce_fusion
  66.1 1.5 fusion.9
  67.7 1.4 fusion.59
  69.1 0.3 copy-done.7
  69.4 1.9 fusion.56
  71.3 1.8 fusion.64
  73.1 1.2 copy.72
  74.3 2.2 convert_element_type.146
  76.5 6.1 %multiply_reduce_fusion = (f32[64]{0:T(128)S(1)}, f32[64,2304]{1,0:T(8,128)S(1)}) fusion(bf16[64,2304]{1,0:T(8,128)(2,1)} %convert_element_type.146, bf16[2304,2304]{1,0:T(8,128)(2,1)} %param.22, bf16[64,2304]{1,0:T(8,128)(2,1)} %param.14), kind=kOutput, calls=%fused_computation.94 | convolution fusion | flops 680361920 | bytes 11796736 | tf_op jit(solution)/shard_map/dot_general | solution.py:152
  82.6 0.8 copy-done.3
  83.6 0.7 copy-done.5
  84.3 1.1 broadcast_in_dim.163
  85.4 2.7 reshape.483
  88.1 1.4 convolution_convert_fusion.2
  89.5 15.8 %all_to_all.10 = bf16[4,48,2304]{2,1,0:T(8,128)(2,1)} all-to-all(bf16[4,48,2304]{2,1,0:T(8,128)(2,1)S(1)} %bitcast.215), channel_id=1, replica_groups=mesh['dp'=8,'expert'=4] {'expert'}, dimensions={0} | all-to-all | bytes 1769472 | tf_op jit(solution)/shard_map/all_to_all | solution.py:183
  105.4 1.5 collective-permute-start
  106.8 20.0 %collective-permute-done = bf16[1,192,2304]{2,1,0:T(8,128)(2,1)} collective-permute-done((bf16[1,192,2304]{2,1,0:T(8,128)(2,1)}, bf16[1,192,2304]{2,1,0:T(8,128)(2,1)}, u32[]{:S(2)}, u32[]{:S(2)}) %collective-permute-start) | collective-permute-done | bytes 884768 | tf_op jit(solution)/shard_map/ppermute | solution.py:27
  126.8 1.6 pad_maximum_fusion.2
  128.4 2.1 fusion.63
  130.5 1.5 collective-permute-start.1
  132.0 38.1 %collective-permute-done.1 = bf16[2,192,2304]{2,1,0:T(8,128)(2,1)} collective-permute-done((bf16[2,192,2304]{2,1,0:T(8,128)(2,1)}, bf16[2,192,2304]{2,1,0:T(8,128)(2,1)}, u32[]{:S(2)}, u32[]{:S(2)}) %collective-permute-start.1) | collective-permute-done | bytes 1769504 | tf_op jit(solution)/shard_map/ppermute | solution.py:27
  170.1 2.3 pad_maximum_fusion.1
  172.4 2.4 reverse_select_fusion.1
  174.8 2.4 collective-permute-start.2
  177.2 150.9 %collective-permute-done.2 = bf16[4,192,2304]{2,1,0:T(8,128)(2,1)} collective-permute-done((bf16[4,192,2304]{2,1,0:T(8,128)(2,1)}, bf16[4,192,2304]{2,1,0:T(8,128)(2,1)}, u32[]{:S(2)}, u32[]{:S(2)}) %collective-permute-start.2) | collective-permute-done | bytes 3538976 | tf_op jit(solution)/shard_map/ppermute | solution.py:27
  328.2 3.7 pad_maximum_fusion
  331.9 4.3 reverse_select_fusion
  336.2 10.5 %fusion.15 = f32[1536,720]{0,1:T(8,128)} fusion(bf16[1536,2304]{1,0:T(8,128)(2,1)} %bitcast.212, bf16[1,2,2304,720]{2,3,1,0:T(8,128)(2,1)} %param.26), kind=kOutput, calls=%fused_computation.29 | convolution fusion | flops 5096079360 | bytes 14819328 | tf_op jit(solution)/shard_map/dot_general | solution.py:186
  346.7 20.1 %convolution_convert_fusion = bf16[1536,2304]{1,0:T(8,128)(2,1)} fusion(bf16[1,720,2304]{2,1,0:T(8,128)(2,1)S(1)} %copy-done, f32[1536,720]{0,1:T(8,128)} %fusion.15, bf16[1536,2304]{1,0:T(8,128)(2,1)} %bitcast.213, bf16[1,2,2304,720]{2,3,1,0:T(8,128)(2,1)} %param.26), kind=kOutput, calls=%fused_computation.1 | convolution fusion | flops 10202333184 | bytes 25214976 | tf_op jit(solution)/shard_map/dot_general | solution.py:190
  368.2 2.3 fusion
  370.5 126.3 %reduce-scatter.2.cloned.1.call-done = bf16[192,2304]{1,0:T(8,128)(2,1)} async-done(((bf16[1536,2304]{1,0:T(8,128)(2,1)}), bf16[192,2304]{1,0:T(8,128)(2,1)}) %reduce-scatter.2.cloned.1.call-update) | async-done | bytes 884752 | tf_op jit(solution)/shard_map/reduce_scatter | solution.py:189
  496.8 4.4 all-to-all-start.1
  501.3 1.1 fusion.116
  502.5 11.5 %all-to-all-done.1 = bf16[4,48,2304]{2,1,0:T(8,128)(2,1)} async-done(((bf16[4,48,2304]{2,1,0:T(8,128)(2,1)}), bf16[4,48,2304]{2,1,0:T(8,128)(2,1)}, u32[]{:S(2)}, u32[]{:S(2)}) %all-to-all-start.1) | async-done | bytes 884768 | tf_op jit(solution)/shard_map/all_to_all | solution.py:195
  514.0 2.5 bitcast_convert_fusion
  516.5 4.0 gather_fusion
  520.5 2.9 gather.7
  523.5 1.4 copy_select_fusion
  524.9 2.0 fusion.73
  (58 shorter events, 2.0 us)
Async XLA Ops:
  7.2 339.5 %copy-start = (bf16[1,720,2304]{2,1,0:T(8,128)(2,1)S(1)}, bf16[1,720,2304]{2,1,0:T(8,128)(2,1)}, u32[]{:S(2)}) copy-start(bf16[1,720,2304]{2,1,0:T(8,128)(2,1)} %param.27) | copy-start | bytes 9953284
  7.2 42.6 %all-gather.2.cloned.1.call-start = ((), (), s32[]{:S(2)}) async-start(), calls=%async_computation.3 | async-start | bytes 5898240 | tf_op jit(solution)/shard_map/all_gather | solution.py:141
  7.9 488.9 %reduce-scatter.2.cloned.1.call-start = ((), (), s32[]{:S(2)}) async-start(), calls=%async_computation.4 | async-start | bytes 7962624 | tf_op jit(solution)/shard_map/reduce_scatter | solution.py:189
  28.7 7.2 %copy-start.12 = (s32[64,2]{0,1:T(2,128)S(1)}, s32[64,2]{0,1:T(2,128)}, u32[]{:S(2)}) copy-start(s32[64,2]{0,1:T(2,128)} %param.25) | copy-start | bytes 1540
  36.2 3.1 copy-start.2
  36.2 3.1 copy-start.4
  38.3 1.0 copy-start.8
  40.2 2.2 copy-start.1
  63.2 4.4 slice-start
  63.2 4.4 slice-start.1
  66.1 1.7 copy-start.6
  67.7 1.7 copy-start.7
  69.4 1.9 copy-start.9
  69.4 1.9 copy-start.10
  76.5 7.0 %copy-start.13 = (f32[2304]{0:T(1024)S(1)}, f32[2304]{0:T(1024)}, u32[]{:S(2)}) copy-start(f32[2304]{0:T(1024)} %param.23) | copy-start | bytes 27652
  82.6 0.8 copy-start.3
  83.6 0.7 copy-start.5
  105.4 21.5 %collective-permute-start = (bf16[1,192,2304]{2,1,0:T(8,128)(2,1)}, bf16[1,192,2304]{2,1,0:T(8,128)(2,1)}, u32[]{:S(2)}, u32[]{:S(2)}) collective-permute-start(bf16[1,192,2304]{2,1,0:T(8,128)(2,1)} %bitcast.29), channel_id=1, source_target_pairs={{0,4},{4,0},{8,12},{12,8},{16,20},{20,16},{24,28},{28,24},{1,5},{5... | collective-permute-start | bytes 2654216 | tf_op jit(solution)/shard_map/ppermute | solution.py:27
  130.5 39.6 %collective-permute-start.1 = (bf16[2,192,2304]{2,1,0:T(8,128)(2,1)}, bf16[2,192,2304]{2,1,0:T(8,128)(2,1)}, u32[]{:S(2)}, u32[]{:S(2)}) collective-permute-start(bf16[2,192,2304]{2,1,0:T(8,128)(2,1)} %get-tuple-element.12), channel_id=1, source_target_pairs={{0,8},{4,12},{8,0},{12,4},{16,24},{20,28},{24,16},{28,20},{1,9},{5... | collective-permute-start | bytes 5308424 | tf_op jit(solution)/shard_map/ppermute | solution.py:27
  174.8 153.4 %collective-permute-start.2 = (bf16[4,192,2304]{2,1,0:T(8,128)(2,1)}, bf16[4,192,2304]{2,1,0:T(8,128)(2,1)}, u32[]{:S(2)}, u32[]{:S(2)}) collective-permute-start(bf16[4,192,2304]{2,1,0:T(8,128)(2,1)} %bitcast.35), channel_id=1, source_target_pairs={{0,16},{4,20},{8,24},{12,28},{16,0},{20,4},{24,8},{28,12},{1,17},{... | collective-permute-start | bytes 10616840 | tf_op jit(solution)/shard_map/ppermute | solution.py:27
  366.8 134.5 %copy-start.11 = (bf16[2304,4]{0,1:T(4,128)(2,1)S(1)}, bf16[2304,4]{0,1:T(4,128)(2,1)}, u32[]{:S(2)}) copy-start(bf16[2304,4]{0,1:T(4,128)(2,1)} %param.24) | copy-start | bytes 55300
  496.8 17.2 %all-to-all-start.1 = ((bf16[4,48,2304]{2,1,0:T(8,128)(2,1)}), bf16[4,48,2304]{2,1,0:T(8,128)(2,1)}, u32[]{:S(2)}, u32[]{:S(2)}) async-start(bf16[4,48,2304]{2,1,0:T(8,128)(2,1)} %bitcast.218), calls=%async_computation.2 | async-start | bytes 1769472 | tf_op jit(solution)/shard_map/all_to_all | solution.py:195
Sparse Core Ops, SparseCore 0:
  9.5 40.1 all-gather.1
  366.9 129.8 reduce-scatter.1
